TPU v7x, 512 devices: a whole 4x4x16 slice. The times are simulated.
512 devices in a mesh: kv: 8 (over y, core), pages: 64 (over x, z).
Axes of the slice: x: 4, y: 4, z: 16, core: 2. Of those that a mesh axis runs over, the one named last changes fastest.
Arguments:
- tokens: int32 [2, 64], replicated, may hold values from 0 to 31999
- prompt_len: int32 [8], replicated, may hold values from 193 to 8192, as said below
- page_table: int32 [8, 64], replicated, may hold values from -1 to 511, as said below
- parents: int32 [2, 64], replicated, may hold values from 0 to 63, as said below
- embedding: bfloat16 [32000, 7168], P('kv', 'pages'), may hold values from -6 to 6
- norm_gain: bfloat16 [7168], P('pages'), may hold values from 0.099609375 to 1.8984375
- w_qkv: bfloat16 [7168, 9216], P('pages', 'kv'), may hold values from -0.0625 to 0.0625
- w_out: bfloat16 [7168, 7168], P('kv', 'pages'), may hold values from -0.8984375 to 0.8984375
- history: bfloat16 [2, 64, 13, 1024], P(None, None, None, 'kv'), may hold values from -6 to 6
- kv_pool: bfloat16 [2, 512, 128, 1024], P(None, 'pages', None, 'kv'), may hold values from -400 to 400
Outputs:
- hidden: bfloat16 [2, 64, 7168], P(None, None, 'pages')
- history_out: bfloat16 [2, 64, 15, 1024], P(None, None, None, 'kv')
Inputs may be any that keep to these rules, and one draw needn't show every extreme that they name: `prompt_len`: each prompt is either long, within 512 tokens below 8192, or short, within 64 tokens below 256; some group's prompt has exactly 8192 tokens. For j below prompt_len[g] / 128 rounded up, page_table[g, j] is the slot holding tokens j * 128 to j * 128 + 127 of group g's prompt; no slot is named twice; all other entries are -1. parents[t, b] is a beam of b's group; at the first step the first and the last beam of every group continue their own history.
All inputs are finite; a program needn't handle non-finite values.
Results may differ from a plain program's by a relative error of at most 0.015.
The roundings to bfloat16 on the way count: a program that leaves them out, or rounds other values in their place, can miss the bound.
Values may be sent and summed in bfloat16 or wider, within the bound.
No kernel may reach another device: no remote copies, remote signals or barrier semaphores. Data moves between devices by JAX's collectives and lax.ppermute only.
A program may use at most 128 MiB of HBM per device.

v0:
```python
import jax
import jax.numpy as jnp
from jax import lax
from jax.sharding import PartitionSpec as P

D = 7168
KV_HEADS = 8
HEAD_DIM = 128
GROUPS = 8
BEAMS = 8
PRIOR = 13
PAGE = 128
PER_KV = 7
HISTORY = 15
MAX_PAGES = 64
THETA = 5000000.0
EPSILON = 1e-05
NEGATIVE = -1e30


def merged(part, axis, combine):
    gathered = jax.tree.map(lambda a: lax.all_gather(a, axis), part)

    def take(source):
        return jax.tree.map(lambda a: lax.dynamic_index_in_dim(a, source, 0, False), gathered)

    return lax.fori_loop(
        1, lax.axis_size(axis), lambda source, state: combine(state, take(source)), take(0)
    )


def rotate(values, positions):
    half_dim = HEAD_DIM // 2
    frequency = THETA ** (-(2.0 * jnp.arange(half_dim, dtype=jnp.float32)) / HEAD_DIM)
    angles = positions.astype(jnp.float32)[:, None] * frequency[None, :]
    cosine = jnp.cos(angles)[:, None, None, :]
    sine_part = jnp.sin(angles)[:, None, None, :]
    lower_part = values[..., :half_dim]
    upper_part = values[..., half_dim:]
    return jnp.concatenate(
        [
            lower_part * cosine - upper_part * sine_part,
            upper_part * cosine + lower_part * sine_part,
        ],
        axis=-1,
    )


def finish_rows(summed, norm_sums, row_ids, prompt_len, num_seqs, local_heads):
    inverse_rms = lax.rsqrt(norm_sums / D + EPSILON)
    projected = (summed * inverse_rms[:, None]).reshape(-1, local_heads, PER_KV + 2, HEAD_DIM)
    positions = jnp.take(prompt_len, row_ids % num_seqs // BEAMS) + PRIOR + row_ids // num_seqs
    turned = rotate(projected[:, :, : PER_KV + 1], positions)
    return jnp.concatenate([turned, projected[:, :, PER_KV + 1 :]], axis=2).astype(jnp.bfloat16)


def combine(earlier, later):
    peak = jnp.maximum(earlier[0], later[0])
    weight_one = jnp.exp(earlier[0] - peak)
    weight_two = jnp.exp(later[0] - peak)
    return (
        peak,
        earlier[1] * weight_one + later[1] * weight_two,
        earlier[2] * weight_one[:, None] + later[2] * weight_two[:, None],
    )


def per_device(
    tokens, prompt_len, page_table, parents, embedding, norm_gain, w_qkv, w_out, history, kv_pool
):
    num_steps, num_seqs = tokens.shape
    row_count = num_steps * num_seqs
    local_heads = KV_HEADS // lax.axis_size("kv")
    kv_width = local_heads * HEAD_DIM
    inv_root = 1.0 / jnp.sqrt(jnp.float32(HEAD_DIM))
    vocab_local = embedding.shape[0]
    local_ids = tokens.reshape(-1) - lax.axis_index("kv") * vocab_local
    inside = (local_ids >= 0) & (local_ids < vocab_local)
    picked = jnp.take(embedding, jnp.clip(local_ids, 0, vocab_local - 1), axis=0)
    found = jnp.where(inside[:, None], picked.astype(jnp.float32), 0.0)
    embedded = lax.psum(found.astype(jnp.bfloat16), "kv")
    widened = embedded.astype(jnp.float32)
    squares = jnp.sum(widened * widened, axis=1)
    normed = (widened * norm_gain.astype(jnp.float32)).astype(jnp.bfloat16)
    partial_value = jnp.dot(normed, w_qkv, preferred_element_type=jnp.float32)
    summed, norm_sums = lax.psum((partial_value, squares), "pages")
    projected = finish_rows(
        summed, norm_sums, jnp.arange(row_count, dtype=jnp.int32), prompt_len, num_seqs, local_heads
    )
    queries = projected[:, :, :PER_KV]
    fresh_kv = jnp.stack([projected[:, :, PER_KV], projected[:, :, PER_KV + 1]]).reshape(
        2, num_steps, num_seqs, kv_width
    )
    buffer = jnp.concatenate(
        [history, jnp.zeros((2, num_seqs, num_steps, kv_width), jnp.bfloat16)], axis=2
    )
    snapshots = []
    for step_index in range(num_steps):
        buffer = jnp.take(buffer, parents[step_index], axis=1)
        buffer = buffer.at[:, :, PRIOR + step_index].set(fresh_kv[:, step_index])
        snapshots.append(buffer)
    stacked = jnp.stack(snapshots)
    tail_keys = stacked[:, 0].reshape(num_steps, num_seqs, HISTORY, local_heads, HEAD_DIM)
    tail_vals = stacked[:, 1].reshape(num_steps, num_seqs, HISTORY, local_heads, HEAD_DIM)
    step_query = queries.reshape(num_steps, num_seqs, local_heads, PER_KV, HEAD_DIM)
    tail_len = PRIOR + 1 + jnp.arange(num_steps, dtype=jnp.int32)
    tail_valid = (jnp.arange(HISTORY, dtype=jnp.int32)[None, :] < tail_len[:, None])[
        :, None, None, None, :
    ]
    tail_scores = (
        jnp.einsum("tbkhd,tblkd->tbkhl", step_query, tail_keys, preferred_element_type=jnp.float32)
        * inv_root
    )
    tail_scores = jnp.where(tail_valid, tail_scores, NEGATIVE)
    tail_peak = jnp.max(tail_scores, axis=-1)
    tail_exp = jnp.where(tail_valid, jnp.exp(tail_scores - tail_peak[..., None]), 0.0)
    tail_total = jnp.sum(tail_exp, axis=-1)
    tail_acc = jnp.einsum(
        "tbkhl,tblkd->tbkhd",
        tail_exp.astype(jnp.bfloat16),
        tail_vals,
        preferred_element_type=jnp.float32,
    )
    tail_part = (tail_peak.reshape(-1), tail_total.reshape(-1), tail_acc.reshape(-1, HEAD_DIM))
    slot_rows = kv_pool.shape[1]
    slot_ids = lax.axis_index("pages") * slot_rows + jnp.arange(slot_rows, dtype=jnp.int32)
    matches = page_table[:, :, None] == slot_ids[None, None, :]
    slot_used = jnp.any(matches, axis=(0, 1))
    owner_group = jnp.sum(
        jnp.where(matches, jnp.arange(GROUPS, dtype=jnp.int32)[:, None, None], 0), axis=(0, 1)
    )
    page_number = jnp.sum(
        jnp.where(matches, jnp.arange(MAX_PAGES, dtype=jnp.int32)[None, :, None], 0), axis=(0, 1)
    )
    length = jnp.take(prompt_len, owner_group)
    live_tok = slot_used[:, None] & (
        page_number[:, None] * PAGE + jnp.arange(PAGE, dtype=jnp.int32)[None, :] < length[:, None]
    )
    live_full = live_tok[None, :, None, :]
    grouped = queries.reshape(num_steps, GROUPS, BEAMS, local_heads, PER_KV, HEAD_DIM)
    chosen = jnp.take(grouped, owner_group, axis=1)
    query_rows = num_steps * BEAMS * PER_KV
    chosen = jnp.transpose(chosen, (3, 1, 0, 2, 4, 5)).reshape(
        local_heads, slot_rows, query_rows, HEAD_DIM
    )
    page_keys = jnp.transpose(
        kv_pool[0].reshape(slot_rows, PAGE, local_heads, HEAD_DIM), (2, 0, 1, 3)
    )
    page_vals = jnp.transpose(
        kv_pool[1].reshape(slot_rows, PAGE, local_heads, HEAD_DIM), (2, 0, 1, 3)
    )
    scores = (
        jnp.einsum("ksqd,kspd->ksqp", chosen, page_keys, preferred_element_type=jnp.float32)
        * inv_root
    )
    scores = jnp.where(live_full, scores, NEGATIVE)
    slot_peak = jnp.max(scores, axis=-1)
    slot_exp = jnp.where(live_full, jnp.exp(scores - slot_peak[..., None]), 0.0)
    slot_total = jnp.sum(slot_exp, axis=-1)
    slot_acc = jnp.einsum(
        "ksqp,kspd->ksqd",
        slot_exp.astype(jnp.bfloat16),
        page_vals,
        preferred_element_type=jnp.float32,
    )
    member = (owner_group[:, None] == jnp.arange(GROUPS, dtype=jnp.int32)[None, :]) & slot_used[
        :, None
    ]
    spread = jnp.where(member[None, :, :, None], slot_peak[:, :, None, :], NEGATIVE)
    group_peak = jnp.max(spread, axis=1)
    slot_base = jnp.take(group_peak, owner_group, axis=1)
    weight = jnp.where(slot_used[None, :, None], jnp.exp(slot_peak - slot_base), 0.0)
    member_f = member.astype(jnp.float32)
    group_total = jnp.einsum(
        "sg,ksq->kgq", member_f, slot_total * weight, precision=lax.Precision.HIGHEST
    )
    group_acc = jnp.einsum(
        "sg,ksqd->kgqd", member_f, slot_acc * weight[..., None], precision=lax.Precision.HIGHEST
    )
    order_small = (2, 1, 3, 0, 4)
    peak_rows = jnp.transpose(
        group_peak.reshape(local_heads, GROUPS, num_steps, BEAMS, PER_KV), order_small
    )
    total_rows = jnp.transpose(
        group_total.reshape(local_heads, GROUPS, num_steps, BEAMS, PER_KV), order_small
    )
    acc_rows = jnp.transpose(
        group_acc.reshape(local_heads, GROUPS, num_steps, BEAMS, PER_KV, HEAD_DIM),
        (2, 1, 3, 0, 4, 5),
    )
    local_part = (peak_rows.reshape(-1), total_rows.reshape(-1), acc_rows.reshape(-1, HEAD_DIM))
    joined = merged(local_part, "pages", combine)
    complete = combine(joined, tail_part)
    attended = (complete[2] / complete[1][:, None]).astype(jnp.bfloat16)
    flat_heads = attended.reshape(row_count, local_heads * PER_KV * HEAD_DIM)
    head_terms = jnp.dot(flat_heads, w_out, preferred_element_type=jnp.float32)
    mixed_out = lax.psum(head_terms.astype(jnp.bfloat16), "kv").astype(jnp.float32) + widened
    return (mixed_out.astype(jnp.bfloat16).reshape(num_steps, num_seqs, -1), buffer)


def solution(mesh):
    placed = (
        P(),
        P(),
        P(),
        P(),
        P("kv", "pages"),
        P("pages"),
        P("pages", "kv"),
        P("kv", "pages"),
        P(None, None, None, "kv"),
        P(None, "pages", None, "kv"),
    )
    return jax.shard_map(
        per_device,
        mesh=mesh,
        in_specs=placed,
        out_specs=(P(None, None, "pages"), P(None, None, None, "kv")),
        check_vma=False,
    )
```

profile of v0, /device:TPU:2, one launch (start us, length us, event | category | flops | bytes accessed | tf_op | source)
XLA Modules:
  0.0 760.0 jit_solution(2022923756878189014)
XLA Ops:
  9.6 1.9 copy.93
  12.4 25.9 %psum.28 = bf16[128,112]{0,1:T(8,128)(2,1)S(1)} all-reduce(bf16[128,112]{0,1:T(8,128)(2,1)S(1)} %select_convert_fusion), channel_id=1, replica_groups=mesh['kv'=8,'pages'=64] {'kv'}, use_global_device_ids=true, to_apply=%region_3.4 | all-reduce | flops 14336 | bytes 57344 | tf_op jit(solution)/shard_map/psum | solution.py:81
  41.4 1.6 fusion.63
  44.3 128.2 %psum.30 = f32[128]{0:T(128)S(1)} all-reduce(f32[128]{0:T(128)S(1)} %fusion.34), channel_id=1, replica_groups=mesh['kv'=8,'pages'=64] {'pages'}, use_global_device_ids=true, to_apply=%region_6.7 | all-reduce | flops 128 | bytes 1024 | tf_op jit(solution)/shard_map/psum | solution.py:86
  172.6 5.0 fusion.54
  177.9 131.7 %all-reduce.3.cloned.1.call-done = f32[128,1152]{1,0:T(8,128)} async-done(((f32[128,1152]{1,0:T(8,128)}), f32[128,1152]{1,0:T(8,128)}) %all-reduce.3.cloned.1.call-update) | async-done | bytes 589840 | tf_op jit(solution)/shard_map/psum | solution.py:86
  317.3 1.4 copy.106
  319.9 1.6 gather_fusion.4
  323.3 80.6 %all-gather = f32[64,1,896]{2,1,0:T(1,128)S(1)} all-gather(f32[1,1,896]{2,1,0:T(1,128)S(1)} %reshape.757), channel_id=1, replica_groups=mesh['kv'=8,'pages'=64] {'pages'}, dimensions={0}, use_global_device_ids=true | all-gather | bytes 232960 | tf_op jit(solution)/shard_map/all_gather | solution.py:22
  404.6 82.0 %all-gather.1 = f32[64,1,896]{2,1,0:T(1,128)S(1)} all-gather(f32[1,1,896]{2,1,0:T(1,128)S(1)} %reshape.759), channel_id=1, replica_groups=mesh['kv'=8,'pages'=64] {'pages'}, dimensions={0}, use_global_device_ids=true | all-gather | bytes 232960 | tf_op jit(solution)/shard_map/all_gather | solution.py:22
  489.3 1.6 gather_fusion.5
  493.7 88.1 %all-gather.4.cloned.1.call-done = f32[64,896,128]{2,1,0:T(8,128)} async-done(((f32[1,896,128]{2,1,0:T(8,128)}), f32[64,896,128]{2,1,0:T(8,128)}) %all-gather.4.cloned.1.call-update) | async-done | bytes 29360144 | tf_op jit(solution)/shard_map/all_gather | solution.py:22
  582.9 142.8 %while.21 = (s32[]{:T(128)}, f32[896]{0:T(1024)S(1)}, f32[896]{0:T(1024)S(1)}, f32[896,128]{1,0:T(8,128)S(1)}, f32[64,896]{1,0:T(8,128)}, /*index=5*/f32[64,896]...) while((s32[]{:T(128)}, f32[896]{0:T(1024)S(1)}, f32[896]{0:T(1024)S(1)}, ...), condition=%wide.region_11.12_spmd, body=%wide.region_10.11_spmd.sunk | while | flops 349445 | bytes 1426575 | solution.py:27
  583.7 1.4 fusion.71
  586.0 1.4 fusion.71
  588.2 1.4 fusion.71
  590.5 1.4 fusion.71
  592.8 1.4 fusion.71
  595.0 1.4 fusion.71
  597.3 1.4 fusion.71
  599.6 1.4 fusion.71
  601.8 1.4 fusion.71
  604.1 1.4 fusion.71
  606.4 1.4 fusion.71
  608.6 1.4 fusion.71
  610.9 1.4 fusion.71
  613.2 1.4 fusion.71
  615.4 1.4 fusion.71
  617.7 1.4 fusion.71
  620.0 1.4 fusion.71
  622.2 1.4 fusion.71
  624.5 1.4 fusion.71
  626.8 1.4 fusion.71
  629.0 1.4 fusion.71
  631.3 1.4 fusion.71
  633.6 1.4 fusion.71
  635.8 1.4 fusion.71
  638.1 1.4 fusion.71
  640.4 1.4 fusion.71
  642.6 1.4 fusion.71
  644.9 1.4 fusion.71
  647.2 1.4 fusion.71
  649.4 1.4 fusion.71
  651.7 1.4 fusion.71
  654.0 1.4 fusion.71
  656.2 1.4 fusion.71
  658.5 1.4 fusion.71
  660.8 1.4 fusion.71
  663.0 1.4 fusion.71
  665.3 1.4 fusion.71
  667.6 1.4 fusion.71
  669.8 1.4 fusion.71
  672.1 1.4 fusion.71
  678.9 1.4 fusion.71
  681.2 1.4 fusion.71
  690.2 1.4 fusion.71
  692.5 1.4 fusion.71
  701.6 1.4 fusion.71
  703.8 1.4 fusion.71
  710.6 1.4 fusion.71
  712.9 1.4 fusion.71
  722.0 1.4 fusion.71
  724.2 1.4 fusion.71
  727.5 24.9 %psum.31 = bf16[128,112]{0,1:T(8,128)(2,1)S(1)} all-reduce(bf16[128,112]{0,1:T(8,128)(2,1)S(1)} %convolution_convert_fusion), channel_id=1, replica_groups=mesh['kv'=8,'pages'=64] {'kv'}, use_global_device_ids=true, to_apply=%region_14.16 | all-reduce | flops 14336 | bytes 57344 | tf_op jit(solution)/shard_map/psum | solution.py:197
  (231 shorter events, 97.5 us)
Async XLA Ops:
  7.2 31.1 %copy-start = (bf16[112,1152]{1,0:T(8,128)(2,1)S(1)}, bf16[112,1152]{1,0:T(8,128)(2,1)}, u32[]{:S(2)}) copy-start(bf16[112,1152]{1,0:T(8,128)(2,1)} %param.24) | copy-start | bytes 774148
  7.2 302.5 %all-reduce.3.cloned.1.call-start = ((), (), s32[]{:S(2)}) async-start(), calls=%async_computation | async-start | bytes 1179648 | tf_op jit(solution)/shard_map/psum | solution.py:86
  39.5 542.4 %all-gather.4.cloned.1.call-start = ((), (), s32[]{:S(2)}) async-start(), calls=%async_computation.1 | async-start | bytes 29818880 | tf_op jit(solution)/shard_map/all_gather | solution.py:22
Sparse Core Ops, SparseCore 0:
  39.6 270.0 all-reduce.2
  317.4 264.3 all-gather.3
where the time goes:
time: 768 us; the launch traced here: 760 us
  blocking collectives  342 us (45%)
  waiting for transfers between devices  220 us (29%)
  other arithmetic  104 us (14%)
  local copies, waits for them, and re-layouts  71.8 us (9%)
  between operations  14.5 us (2%)
    all_gather x2, blocking collectives, merged(): gathered = jax.tree.map(lambda a: lax.all_gather(a, axis), part)  163 us
    psum x1, waiting for transfers between devices, per_device(): summed, norm_sums = lax.psum((partial_value, squares), 'pages')  132 us
    psum x1, blocking collectives, per_device(): summed, norm_sums = lax.psum((partial_value, squares), 'pages')  128 us
    add x63, other arithmetic, combine(): earlier[2] * weight_one[:, None] + later[2] * weight_two[:, None]  89.9 us
    all_gather x1, waiting for transfers between devices, merged(): gathered = jax.tree.map(lambda a: lax.all_gather(a, axis), part)  88.1 us
    dynamic_slice x65, local copies, waits for them, and re-layouts, take(): lax.dynamic_index_in_dim(a, source, 0, False)  50.1 us
    psum x1, blocking collectives, per_device(): embedded = lax.psum(found.astype(jnp.bfloat16), 'kv')  25.9 us
    psum x1, blocking collectives, per_device(): lax.psum(head_terms.astype(jnp.bfloat16), 'kv').astype(jnp.float32)  24.9 us
  transfers between devices with their start and end apart: 2, of which 2 were waited for; matrix products, arithmetic and copies ran while one was open for 3% of the time, Pallas kernels for 0%

commit v1 on v0

--- a/solution.py
+++ b/solution.py
@@ -78,7 +78,8 @@
     inside = (local_ids >= 0) & (local_ids < vocab_local)
     picked = jnp.take(embedding, jnp.clip(local_ids, 0, vocab_local - 1), axis=0)
     found = jnp.where(inside[:, None], picked.astype(jnp.float32), 0.0)
-    embedded = lax.psum(found.astype(jnp.bfloat16), "kv")
+    fill_values = lambda mat: jnp.sum(jax.lax.all_gather(mat, "kv"), axis=0)
+    embedded = fill_values(found.astype(jnp.bfloat16))
     widened = embedded.astype(jnp.float32)
     squares = jnp.sum(widened * widened, axis=1)
     normed = (widened * norm_gain.astype(jnp.float32)).astype(jnp.bfloat16)

time: 768 us -> 757 us (0.986)
  blocking collectives: 342 us -> 329 us
    psum x1 -> x0, blocking collectives: 25.9 us -> none  [per_device(): embedded = lax.psum(found.astype(jnp.bfloat16), 'kv')]
    all_gather x0 -> x1, blocking collectives: none -> 13.3 us  [per_device(): fill_values = lambda mat: jnp.sum(jax.lax.all_gather(mat, 'kv'), axis=0)]
where the time goes in v1:
time: 757 us; the launch traced here: 749 us
  blocking collectives  329 us (43%)
  waiting for transfers between devices  222 us (29%)
  other arithmetic  104 us (14%)
  local copies, waits for them, and re-layouts  71.8 us (9%)
  between operations  14.5 us (2%)
    all_gather x2, blocking collectives, merged(): gathered = jax.tree.map(lambda a: lax.all_gather(a, axis), part)  163 us
    psum x1, waiting for transfers between devices, per_device(): summed, norm_sums = lax.psum((partial_value, squares), 'pages')  134 us
    psum x1, blocking collectives, per_device(): summed, norm_sums = lax.psum((partial_value, squares), 'pages')  128 us
    add x63, other arithmetic, combine(): earlier[2] * weight_one[:, None] + later[2] * weight_two[:, None]  89.9 us
    all_gather x1, waiting for transfers between devices, merged(): gathered = jax.tree.map(lambda a: lax.all_gather(a, axis), part)  88.1 us
    dynamic_slice x65, local copies, waits for them, and re-layouts, take(): lax.dynamic_index_in_dim(a, source, 0, False)  50.1 us
    psum x1, blocking collectives, per_device(): lax.psum(head_terms.astype(jnp.bfloat16), 'kv').astype(jnp.float32)  24.9 us
  transfers between devices with their start and end apart: 2, of which 2 were waited for; matrix products, arithmetic and copies ran while one was open for 3% of the time, Pallas kernels for 0%

profile of v1, /device:TPU:2, one launch (start us, length us, event | category | flops | bytes accessed | tf_op | source)
XLA Modules:
  0.0 749.3 jit_solution(4908775873403111483)
XLA Ops:
  9.6 1.9 copy.118
  12.4 13.3 %all_gather.13 = bf16[8,128,112]{1,2,0:T(8,128)(2,1)S(1)} all-gather(bf16[1,128,112]{1,2,0:T(8,128)(2,1)S(1)} %select_convert_fusion), channel_id=1, replica_groups=mesh['kv'=8,'pages'=64] {'kv'}, dimensions={0}, use_global_device_ids=true | all-gather | bytes 258048 | tf_op jit(solution)/shard_map/all_gather | solution.py:81
  28.9 1.6 fusion.63
  31.8 128.1 %psum.22 = f32[128]{0:T(128)S(1)} all-reduce(f32[128]{0:T(128)S(1)} %fusion.34), channel_id=1, replica_groups=mesh['kv'=8,'pages'=64] {'pages'}, use_global_device_ids=true, to_apply=%region_6.7 | all-reduce | flops 128 | bytes 1024 | tf_op jit(solution)/shard_map/psum | solution.py:87
  160.0 5.0 fusion.54
  165.3 133.7 %all-reduce.3.cloned.1.call-done = f32[128,1152]{1,0:T(8,128)} async-done(((f32[128,1152]{1,0:T(8,128)}), f32[128,1152]{1,0:T(8,128)}) %all-reduce.3.cloned.1.call-update) | async-done | bytes 589840 | tf_op jit(solution)/shard_map/psum | solution.py:87
  306.6 1.4 copy.133
  309.2 1.6 gather_fusion.4
  312.7 80.7 %all-gather = f32[64,1,896]{2,1,0:T(1,128)S(1)} all-gather(f32[1,1,896]{2,1,0:T(1,128)S(1)} %reshape.808), channel_id=1, replica_groups=mesh['kv'=8,'pages'=64] {'pages'}, dimensions={0}, use_global_device_ids=true | all-gather | bytes 232960 | tf_op jit(solution)/shard_map/all_gather | solution.py:22
  394.1 81.9 %all-gather.1 = f32[64,1,896]{2,1,0:T(1,128)S(1)} all-gather(f32[1,1,896]{2,1,0:T(1,128)S(1)} %reshape.810), channel_id=1, replica_groups=mesh['kv'=8,'pages'=64] {'pages'}, dimensions={0}, use_global_device_ids=true | all-gather | bytes 232960 | tf_op jit(solution)/shard_map/all_gather | solution.py:22
  478.6 1.6 gather_fusion.5
  483.0 88.1 %all-gather.4.cloned.1.call-done = f32[64,896,128]{2,1,0:T(8,128)} async-done(((f32[1,896,128]{2,1,0:T(8,128)}), f32[64,896,128]{2,1,0:T(8,128)}) %all-gather.4.cloned.1.call-update) | async-done | bytes 29360144 | tf_op jit(solution)/shard_map/all_gather | solution.py:22
  572.2 142.8 %while.21 = (s32[]{:T(128)}, f32[896]{0:T(1024)S(1)}, f32[896]{0:T(1024)S(1)}, f32[896,128]{1,0:T(8,128)S(1)}, f32[64,896]{1,0:T(8,128)}, /*index=5*/f32[64,896]...) while((s32[]{:T(128)}, f32[896]{0:T(1024)S(1)}, f32[896]{0:T(1024)S(1)}, ...), condition=%wide.region_11.12_spmd, body=%wide.region_10.11_spmd.sunk | while | flops 349445 | bytes 1426575 | solution.py:27
  573.0 1.4 fusion.71
  575.3 1.4 fusion.71
  577.6 1.4 fusion.71
  579.8 1.4 fusion.71
  582.1 1.4 fusion.71
  584.4 1.4 fusion.71
  586.6 1.4 fusion.71
  588.9 1.4 fusion.71
  591.2 1.4 fusion.71
  593.4 1.4 fusion.71
  595.7 1.4 fusion.71
  598.0 1.4 fusion.71
  600.2 1.4 fusion.71
  602.5 1.4 fusion.71
  604.8 1.4 fusion.71
  607.0 1.4 fusion.71
  609.3 1.4 fusion.71
  611.6 1.4 fusion.71
  613.8 1.4 fusion.71
  616.1 1.4 fusion.71
  618.4 1.4 fusion.71
  620.6 1.4 fusion.71
  622.9 1.4 fusion.71
  625.2 1.4 fusion.71
  627.4 1.4 fusion.71
  629.7 1.4 fusion.71
  632.0 1.4 fusion.71
  634.2 1.4 fusion.71
  636.5 1.4 fusion.71
  638.8 1.4 fusion.71
  641.0 1.4 fusion.71
  643.3 1.4 fusion.71
  645.6 1.4 fusion.71
  647.8 1.4 fusion.71
  650.1 1.4 fusion.71
  652.4 1.4 fusion.71
  654.6 1.4 fusion.71
  656.9 1.4 fusion.71
  659.2 1.4 fusion.71
  661.4 1.4 fusion.71
  668.2 1.4 fusion.71
  670.5 1.4 fusion.71
  679.5 1.4 fusion.71
  681.8 1.4 fusion.71
  690.9 1.4 fusion.71
  693.1 1.4 fusion.71
  702.2 1.4 fusion.71
  704.5 1.4 fusion.71
  711.3 1.4 fusion.71
  713.5 1.4 fusion.71
  716.8 24.9 %psum.23 = bf16[128,112]{0,1:T(8,128)(2,1)S(1)} all-reduce(bf16[128,112]{0,1:T(8,128)(2,1)S(1)} %convolution_convert_fusion), channel_id=1, replica_groups=mesh['kv'=8,'pages'=64] {'kv'}, use_global_device_ids=true, to_apply=%region_14.16 | all-reduce | flops 14336 | bytes 57344 | tf_op jit(solution)/shard_map/psum | solution.py:198
  (232 shorter events, 97.5 us)
Async XLA Ops:
  7.2 18.6 %copy-start = (bf16[112,1152]{1,0:T(8,128)(2,1)S(1)}, bf16[112,1152]{1,0:T(8,128)(2,1)}, u32[]{:S(2)}) copy-start(bf16[112,1152]{1,0:T(8,128)(2,1)} %param.24) | copy-start | bytes 774148
  7.2 291.8 %all-reduce.3.cloned.1.call-start = ((), (), s32[]{:S(2)}) async-start(), calls=%async_computation | async-start | bytes 1179648 | tf_op jit(solution)/shard_map/psum | solution.py:87
  26.9 544.2 %all-gather.4.cloned.1.call-start = ((), (), s32[]{:S(2)}) async-start(), calls=%async_computation.1 | async-start | bytes 29818880 | tf_op jit(solution)/shard_map/all_gather | solution.py:22
Sparse Core Ops, SparseCore 0:
  27.1 271.9 all-reduce.2
  306.8 264.3 all-gather.3
